TPU v7x, 32 devices: a whole 2x2x4 slice. The times are simulated.
32 devices in a mesh: dp: 2 (over core), ctx: 4 (over z), expert: 4 (over y, x).
Axes of the slice: x: 2, y: 2, z: 4, core: 2. Of those that a mesh axis runs over, the one named last changes fastest.
Arguments:
- x_in: bfloat16 [4, 64, 8192], P('dp', 'ctx', 'expert'), may hold values from -6 to 6
- z_in: bfloat16 [4, 64, 8192], P('dp', 'ctx', 'expert'), may hold values from -6 to 6
- b_in: bfloat16 [4, 64, 128], P('dp', 'ctx'), may hold values from -0.5 to 0.5
- c_in: bfloat16 [4, 64, 128], P('dp', 'ctx'), may hold values from -0.75 to 0.75
- decay_log: float32 [4, 64, 128], P('dp', 'ctx', 'expert'), may hold values from -2 to 0, as said below
- skip: float32 [128], P('expert'), may hold values from 0.5 to 1.5
- out_weight: bfloat16 [8192, 4096], P('expert', 'ctx'), may hold values from -1 to 1
- moe_gain: float32 [4096], replicated, may hold values from 0.5 to 1.5
- gate_up: bfloat16 [4, 2, 7168, 4096], P('expert', None, ('dp', 'ctx')), may hold values from -0.09375 to 0.09375
- expert_ids: int32 [4, 64, 2], P('dp', ('ctx', 'expert')), may hold values from 0 to 3, as said below
- slot_ids: int32 [4, 64, 2], P('dp', ('ctx', 'expert')), may hold values from 0 to 7, as said below
Outputs:
- mamba_out: bfloat16 [4, 64, 4096], P('dp', ('ctx', 'expert'))
- expert_hidden: bfloat16 [4, 7168, 256], P('expert', ('dp', 'ctx'))
Inputs may be any that keep to these rules, and one draw needn't show every extreme that they name: `decay_log`: its values are negative. `expert_ids`: each token names two different experts. In the rows of one device (streams s with the same s // 2, positions t with the same t // 4) one expert, the same for all devices, is named by exactly 8 rows, and no expert by more than 8 rows. `slot_ids`: in the rows of one device the pairs (expert, slot) are all different.
All inputs are finite; a program needn't handle non-finite values.
Results may differ from a plain program's by a relative error of at most 0.0085.
Values may be sent and summed in bfloat16 or wider, within the bound.
No kernel may reach another device: no remote copies, remote signals or barrier semaphores. Data moves between devices by JAX's collectives and lax.ppermute only.
A program may use at most 128 MiB of HBM per device.

v0:
```python
import jax
import jax.numpy as jnp
from jax import lax
from jax.sharding import PartitionSpec as P

P_SIZE = 64
ALL_AXES = ("dp", "ctx", "expert")


def mixer(x_in, b_in, c_in, decay_log, skip):
    highest = lax.Precision.HIGHEST
    seq_count, total_len, width_in = x_in.shape
    head_count = skip.shape[0]
    state_size = b_in.shape[2]
    chunk = total_len if total_len <= 128 else 64
    chunks = total_len // chunk
    x_float = x_in.astype(jnp.float32).reshape(seq_count, chunks, chunk, head_count, P_SIZE)
    b_float = b_in.astype(jnp.float32).reshape(seq_count, chunks, chunk, state_size)
    c_float = c_in.astype(jnp.float32).reshape(seq_count, chunks, chunk, state_size)
    cum_decay = jnp.cumsum(decay_log.reshape(seq_count, chunks, chunk, head_count), axis=2)
    scores = jnp.einsum("sktn,skun->sktu", c_float, b_float, precision=highest)
    causal = (jnp.arange(chunk)[:, None] >= jnp.arange(chunk)[None, :])[None, None, :, :, None]
    spans = cum_decay[:, :, :, None, :] - cum_decay[:, :, None, :, :]
    kernel = jnp.where(causal, jnp.exp(jnp.where(causal, spans, 0.0)), 0.0) * scores[..., None]
    ssd = jnp.einsum("sktuh,skuhp->skthp", kernel, x_float, precision=highest)
    if chunks > 1:
        final_decay = cum_decay[:, :, -1, :]
        tails = jnp.exp(final_decay[:, :, None, :] - cum_decay)
        states = jnp.einsum("skuh,skuhp,skun->skhpn", tails, x_float, b_float, precision=highest)

        def step(carry, inputs):
            decay_k, state_k = inputs
            return (decay_k[:, :, None, None] * carry + state_k, carry)

        _, incoming = lax.scan(
            step,
            jnp.zeros_like(states[:, 0]),
            (jnp.moveaxis(jnp.exp(final_decay), 1, 0), jnp.moveaxis(states, 1, 0)),
        )
        incoming = jnp.moveaxis(incoming, 0, 1)
        ssd = ssd + jnp.exp(cum_decay)[..., None] * jnp.einsum(
            "sktn,skhpn->skthp", c_float, incoming, precision=highest
        )
    ssd = ssd + skip[None, None, None, :, None] * x_float
    return ssd.reshape(seq_count, total_len, width_in)


def expert_ffn(gate_up, slot_rows):
    both = jnp.einsum("gfd,qd->gfq", gate_up[0], slot_rows, preferred_element_type=jnp.float32)
    return (jax.nn.silu(both[0]) * both[1]).astype(jnp.bfloat16)


def dispatch_routed(partial_value, moe_gain, gate_up, expert_ids, slot_ids, capacity):
    seq_count = partial_value.shape[0]
    model_width = moe_gain.shape[0]
    per_block = expert_ids.shape[1]
    pick_count = expert_ids.shape[2]
    row_count = seq_count * per_block
    ctx_count = lax.axis_size("ctx")
    group_count = lax.axis_size("expert")
    grouped = partial_value.reshape(
        seq_count, ctx_count, group_count, per_block, partial_value.shape[2]
    )
    reduced = lax.psum_scatter(grouped, "expert", scatter_dimension=2, tiled=True).astype(
        jnp.bfloat16
    )
    swapped = lax.all_to_all(reduced, "ctx", split_axis=1, concat_axis=4, tiled=True)
    mamba_out = swapped.reshape(seq_count, per_block, model_width)
    flat = mamba_out.reshape(row_count, model_width).astype(jnp.float32)
    scale = lax.rsqrt(jnp.mean(flat * flat, axis=1, keepdims=True) + 1e-05)
    normed = (flat * scale * moe_gain[None, :]).astype(jnp.bfloat16)
    chosen = expert_ids.reshape(row_count, pick_count)
    placed = slot_ids.reshape(row_count, pick_count)
    match_expert = chosen[:, :, None, None] == jnp.arange(group_count)[None, None, :, None]
    match_slot = placed[:, :, None, None] == jnp.arange(capacity)[None, None, None, :]
    selector = (match_expert & match_slot).astype(jnp.bfloat16)
    outgoing = jnp.einsum(
        "rkec,rd->ecd", selector, normed, preferred_element_type=jnp.float32
    ).astype(jnp.bfloat16)
    arrived = lax.all_to_all(outgoing, "expert", split_axis=0, concat_axis=0, tiled=True)
    piece = lax.all_gather(arrived[None], ("dp", "ctx"), axis=0, tiled=True)
    slot_rows = piece.reshape(-1, piece.shape[3])
    return (mamba_out, expert_ffn(gate_up, slot_rows)[None])


def local(
    x_in, z_in, b_in, c_in, decay_log, skip, out_weight, moe_gain, gate_up, expert_ids, slot_ids
):
    seq_count, block_len, width_in = x_in.shape
    state_size = b_in.shape[2]
    model_width = moe_gain.shape[0]
    col_width = out_weight.shape[1]
    per_block = expert_ids.shape[1]
    pick_count = expert_ids.shape[2]
    dp_count = lax.axis_size("dp")
    ctx_count = lax.axis_size("ctx")
    group_count = lax.axis_size("expert")
    device_count = dp_count * ctx_count * group_count
    row_count = seq_count * per_block
    capacity = max(2, 4 * row_count // group_count)
    packed = jnp.concatenate([x_in, z_in, b_in, c_in], axis=2)
    packed = lax.all_gather(packed, "ctx", axis=1, tiled=True)
    decay_all = lax.all_gather(decay_log, "ctx", axis=1, tiled=True)
    route = jnp.stack([expert_ids, slot_ids], axis=-1)
    routes = lax.all_gather(route[None], ALL_AXES, axis=0, tiled=True)
    packed, decay_all, routes = lax.optimization_barrier((packed, decay_all, routes))
    x_all = packed[:, :, :width_in]
    z_all = packed[:, :, width_in : 2 * width_in]
    b_all = packed[:, :, 2 * width_in : 2 * width_in + state_size]
    c_all = packed[:, :, 2 * width_in + state_size :]
    ssd = mixer(x_all, b_all, c_all, decay_all, skip)
    gated = (ssd * jax.nn.silu(z_all.astype(jnp.float32))).astype(jnp.bfloat16)
    partial_value = jnp.einsum("stk,kd->std", gated, out_weight, preferred_element_type=jnp.float32)
    if device_count * row_count * model_width * 2 > 8 << 20:
        return dispatch_routed(partial_value, moe_gain, gate_up, expert_ids, slot_ids, capacity)
    summed = lax.psum(partial_value, "expert").astype(jnp.bfloat16)
    gathered = lax.all_gather(summed[None], ("dp", "ctx"), axis=0, tiled=True)
    gathered = gathered.reshape(
        dp_count, ctx_count, seq_count, ctx_count, group_count, per_block, col_width
    )
    tokens = jnp.transpose(gathered, (0, 3, 4, 2, 5, 1, 6)).reshape(
        device_count, row_count, model_width
    )
    me = (lax.axis_index("dp") * ctx_count + lax.axis_index("ctx")) * group_count + lax.axis_index(
        "expert"
    )
    mamba_out = lax.dynamic_index_in_dim(tokens, me, axis=0, keepdims=False).reshape(
        seq_count, per_block, model_width
    )
    flat = tokens.reshape(device_count * row_count, model_width).astype(jnp.float32)
    scale = lax.rsqrt(jnp.mean(flat * flat, axis=1, keepdims=True) + 1e-05)
    normed = (flat * scale * moe_gain[None, :]).astype(jnp.bfloat16)
    chosen = routes[..., 0].reshape(device_count, row_count, pick_count)
    placed = routes[..., 1].reshape(device_count, row_count, pick_count)
    target = jnp.arange(device_count)[:, None, None] * capacity + placed
    mine = chosen == lax.axis_index("expert")
    slot_count = device_count * capacity
    hit = mine[..., None] & (target[..., None] == jnp.arange(slot_count))
    selector = jnp.any(hit, axis=2).reshape(device_count * row_count, slot_count)
    dispatched = jnp.einsum(
        "rq,rd->qd", selector.astype(jnp.bfloat16), normed, preferred_element_type=jnp.float32
    ).astype(jnp.bfloat16)
    hidden = expert_ffn(gate_up, dispatched)
    return (mamba_out, hidden[None])


def solution(mesh):
    in_specs = (
        P("dp", "ctx", "expert"),
        P("dp", "ctx", "expert"),
        P("dp", "ctx", None),
        P("dp", "ctx", None),
        P("dp", "ctx", "expert"),
        P("expert"),
        P("expert", "ctx"),
        P(),
        P("expert", None, ("dp", "ctx"), None),
        P("dp", ("ctx", "expert"), None),
        P("dp", ("ctx", "expert"), None),
    )
    out_specs = (P("dp", ("ctx", "expert"), None), P("expert", ("dp", "ctx"), None))
    return jax.shard_map(local, mesh=mesh, in_specs=in_specs, out_specs=out_specs, check_vma=False)
```

profile of v0, /device:TPU:0, one launch (start us, length us, event | category | flops | bytes accessed | tf_op | source)
XLA Modules:
  0.0 197.7 jit_solution(9487829076397545816)
XLA Ops:
  7.2 0.0 all-gather.5.cloned.1.call-start
  7.2 1.7 pad_maximum_fusion
  8.9 0.0 all-gather.5.cloned.1.call-update
  9.0 0.0 all-gather.7.cloned.1.call-start
  9.0 0.7 pad_add_fusion
  9.7 71.7 %all-gather = s32[64,4,2,2]{1,2,0,3:T(2,128)S(1)} all-gather(s32[2,4,2,2]{1,2,0,3:T(2,128)S(1)} %pad_add_fusion), channel_id=2, replica_groups=mesh['dp'=2,'ctx'=4,'expert'=4] {'dp','ctx','expert'}, dimensions={0}, use_global_device_ids=true | all-gather | bytes 4224 | tf_op jit(solution)/shard_map/all_gather | solution.py:105
  81.4 13.3 %all_gather.13 = f32[2,64,32]{2,1,0:T(8,128)S(1)} all-gather(f32[2,16,32]{2,1,0:T(8,128)} %param.15), channel_id=1, replica_groups=mesh['dp'=2,'ctx'=4,'expert'=4] {'ctx'}, dimensions={1}, use_global_device_ids=true | all-gather | bytes 20480 | tf_op jit(solution)/shard_map/all_gather | solution.py:103
  94.8 0.0 all-gather.5.cloned.1.call-done
  94.8 0.9 fusion.37
  95.7 1.2 fusion.42
  96.9 0.1 reduce_window_sum.11
  97.0 0.1 copy.41
  97.1 0.0 copy-start.2
  97.1 1.3 copy.52
  98.4 0.6 copy.53
  99.0 0.0 copy-done.2
  99.0 4.8 %bitcast_add_fusion = f32[2,1,64,32,64]{2,4,3,0,1:T(8,128)} fusion(f32[2,1,64,32,64]{2,4,3,0,1:T(8,128)S(1)} %bitcast.46, bf16[2,64,32,64]{1,3,2,0:T(8,128)(2,1)} %bitcast.49, f32[32]{0:T(128)S(1)} %copy-done.2, f32[2,64,64]{2,1,0:T(8,128)S(1)} %fusion.37, f32[2,64,32]{1,2,0:T(8,128)S(1)} %copy.41, pred[64,64]{1,0:T(8,128)(4,1)S(1)} %iota_compare_fusion.1), kind=kOutput, calls=%fused_computation.11 | convolution fusion | flops 202899456 | bytes 2674816 | tf_op jit(solution)/shard_map/sktuh,skuhp->skthp/dot_general | solution.py:25
  103.8 0.0 copy-start
  103.8 2.3 %copy.54 = f32[2,64,2048]{2,1,0:T(8,128)S(1)} copy(f32[2,64,2048]{1,2,0:T(8,128)} %bitcast.47) | data formatting | bytes 2097152 | tf_op jit(solution)/shard_map/reshape | solution.py:45
  106.1 0.0 copy-done
  106.1 0.0 copy-start.1
  106.1 3.0 %fusion.6 = f32[2,64,1024]{2,1,0:T(8,128)S(1)} fusion(bf16[2048,1024]{1,0:T(8,128)(2,1)} %param.17, f32[2,64,2048]{2,1,0:T(8,128)S(1)} %copy.54, bf16[2,64,4352]{2,1,0:T(8,128)(2,1)S(1)} %copy-done), kind=kOutput, calls=%fused_computation.9 | convolution fusion | flops 538705920 | bytes 6291456 | tf_op jit(solution)/shard_map/stk,kd->std/dot_general | solution.py:113
  109.1 23.6 %all-reduce.1 = bf16[2,64,1024]{2,1,0:T(8,128)(2,1)} all-reduce(f32[2,64,1024]{2,1,0:T(8,128)S(1)} %fusion.6), channel_id=1, replica_groups=mesh['dp'=2,'ctx'=4,'expert'=4] {'expert'}, use_global_device_ids=true, to_apply=%region_1.2 | all-reduce | flops 131072 | bytes 786432 | tf_op jit(solution)/shard_map/psum | solution.py:116
  132.8 0.0 all-gather.7.cloned.1.call-update
  132.8 0.0 copy-done.1
  132.8 0.1 copy.47
  133.0 0.1 copy.48
  133.1 0.1 copy.50
  133.2 0.2 fusion.34
  133.4 26.2 %all-gather.7.cloned.1.call-done = bf16[16,64,1024]{2,1,0:T(8,128)(2,1)} async-done(((bf16[2,64,1024]{2,1,0:T(8,128)(2,1)}), bf16[16,64,1024]{2,1,0:T(8,128)(2,1)}) %all-gather.7.cloned.1.call-update) | async-done | bytes 2097168 | tf_op jit(solution)/shard_map/all_gather | solution.py:117
  159.6 2.7 %reshape.131 = bf16[2,4,2,4,4,4,1024]{6,5,4,3,2,1,0:T(4,128)(2,1)S(1)} reshape(bf16[16,64,1024]{2,1,0:T(8,128)(2,1)} %all-gather.7.cloned.1.call-done) | data formatting | bytes 4194304 | tf_op jit(solution)/shard_map/reshape | solution.py:118
  162.4 2.1 %fusion.3 = f32[2,4,4,2,4]{4,3,2,1,0:T(2,128)S(1)} fusion(bf16[2,4,2,4,4,4,1024]{6,5,4,3,2,1,0:T(4,128)(2,1)S(1)} %reshape.131), kind=kLoop, calls=%fused_computation.6 | loop fusion | flops 3145472 | bytes 2098176 | tf_op jit(solution)/shard_map/reduce_sum | solution.py:131
  164.5 4.2 %copy.61 = bf16[2,4,2,4,4,4,1024]{6,1,5,2,4,3,0:T(4,128)(2,1)} copy(bf16[2,4,2,4,4,4,1024]{6,5,4,3,2,1,0:T(4,128)(2,1)S(1)} %reshape.131) | data formatting | bytes 4194304 | tf_op jit(solution)/shard_map/reshape | solution.py:118
  168.7 4.5 %reshape.132 = bf16[32,8,4096]{2,1,0:T(8,128)(2,1)} reshape(bf16[2,4,4,2,4,4,1024]{6,5,4,3,2,1,0:T(4,128)(2,1)} %bitcast.45) | data formatting | bytes 4194304 | tf_op jit(solution)/shard_map/reshape | solution.py:121
  173.2 0.8 constant_dynamic-slice_fusion
  174.1 0.7 reshape.133
  174.7 2.6 %fusion.5 = bf16[2,4,4,2,4,4,1024]{6,5,4,3,2,1,0:T(4,128)(2,1)S(1)} fusion(f32[4,1024]{1,0:T(4,128)S(1)} %mul.97, f32[2,4,4,2,4]{4,3,2,1,0:T(2,128)S(1)} %add_rsqrt_fusion, bf16[2,4,2,4,4,4,1024]{6,5,4,3,2,1,0:T(4,128)(2,1)S(1)} %reshape.131), kind=kLoop, calls=%fused_computation.8 | loop fusion | flops 4194304 | bytes 4211712 | tf_op jit(solution)/shard_map/convert_element_type | solution.py:132
  177.4 0.9 copy.55
  178.2 9.9 %fusion.16 = f32[2,896,256]{1,2,0:T(8,128)} fusion(bf16[1,2,896,4096]{3,2,1,0:T(8,128)(2,1)} %param.19, bf16[256,4096]{1,0:T(8,128)(2,1)S(1)} %bitcast.48, pred[32,8,256]{2,1,0:T(8,128)(4,1)S(1)} %fusion.34), kind=kOutput, calls=%fused_computation.19 | convolution fusion | flops 4296015872 | bytes 18677760 | tf_op jit(solution)/shard_map/gfd,qd->gfq/dot_general | solution.py:49
  188.2 1.7 fusion.29
  189.9 1.0 copy.51
  (7 shorter events, 0.1 us)
Async XLA Ops:
  7.2 87.6 %all-gather.5.cloned.1.call-start = ((), (), s32[]{:S(2)}) async-start(), calls=%async_computation | async-start | bytes 1392640 | tf_op jit(solution)/shard_map/all_gather | solution.py:102
  9.0 150.7 %all-gather.7.cloned.1.call-start = ((), (), s32[]{:S(2)}) async-start(), calls=%async_computation.1 | async-start | bytes 2359296 | tf_op jit(solution)/shard_map/all_gather | solution.py:117
  97.1 1.9 copy-start.2
  103.8 2.3 %copy-start = (bf16[2,64,4352]{2,1,0:T(8,128)(2,1)S(1)}, bf16[2,64,4352]{2,1,0:T(8,128)(2,1)}, u32[]{:S(2)}) copy-start(bf16[2,64,4352]{2,1,0:T(8,128)(2,1)} %all-gather.5.cloned.1.call-done) | copy-start | bytes 3342340
  106.1 26.7 %copy-start.1 = (f32[4096]{0:T(1024)S(1)}, f32[4096]{0:T(1024)}, u32[]{:S(2)}) copy-start(f32[4096]{0:T(1024)} %param.18) | copy-start | bytes 49156
Sparse Core Ops, SparseCore 0:
  10.1 32.3 all-gather.4
  132.9 26.6 all-gather.6
where the time goes:
time: 198 us
  blocking collectives  109 us (55%)
  waiting for transfers between devices  26.3 us (13%)
  local copies, waits for them, and re-layouts  19.4 us (10%)
  matrix products  18.6 us (9%)
  between operations  14.2 us (7%)
  other arithmetic  10.5 us (5%)
    all_gather x1, blocking collectives, local(): routes = lax.all_gather(route[None], ALL_AXES, axis=0, tiled=True)  71.7 us
    all_gather x1, waiting for transfers between devices, local(): gathered = lax.all_gather(summed[None], ('dp', 'ctx'), axis=0, tiled=True)  26.2 us
    psum x1, blocking collectives, local(): summed = lax.psum(partial_value, 'expert').astype(jnp.bfloat16)  23.6 us
    all_gather x1, blocking collectives, local(): decay_all = lax.all_gather(decay_log, 'ctx', axis=1, tiled=True)  13.3 us
    dot_general x1, matrix products, expert_ffn(): jnp.einsum('gfd,qd->gfq', gate_up[0], slot_rows, preferred_element_type=j...  9.91 us
    reshape x2, local copies, waits for them, and re-layouts, local(): gathered.reshape(dp_count, ctx_count, seq_count, ctx_count, group_count,...  6.91 us
    dot_general x1, matrix products, mixer(): ssd = jnp.einsum('sktuh,skuhp->skthp', kernel, x_float, precision=highest)  4.79 us
    reshape x1, local copies, waits for them, and re-layouts, local(): jnp.transpose(gathered, (0, 3, 4, 2, 5, 1, 6))  4.48 us
  transfers between devices with their start and end apart: 2, of which 1 were waited for; matrix products, arithmetic and copies ran while one was open for 1% of the time, Pallas kernels for 0%

commit v1 on v0

--- a/solution.py
+++ b/solution.py
@@ -113,7 +113,7 @@
     partial_value = jnp.einsum("stk,kd->std", gated, out_weight, preferred_element_type=jnp.float32)
     if device_count * row_count * model_width * 2 > 8 << 20:
         return dispatch_routed(partial_value, moe_gain, gate_up, expert_ids, slot_ids, capacity)
-    summed = lax.psum(partial_value, "expert").astype(jnp.bfloat16)
+    summed = jnp.sum(lax.all_gather(partial_value, axis_name="expert"), axis=0).astype(jnp.bfloat16)
     gathered = lax.all_gather(summed[None], ("dp", "ctx"), axis=0, tiled=True)
     gathered = gathered.reshape(
         dp_count, ctx_count, seq_count, ctx_count, group_count, per_block, col_width

time: 198 us -> 213 us (1.076)
  waiting for transfers between devices: 26.3 us -> 60.2 us
  blocking collectives: 109 us -> 85 us
    all_gather x0 -> x1, waiting for transfers between devices: none -> 31.4 us  [local(): lax.all_gather(partial_value, axis_name='expert')]
    psum x1 -> x0, blocking collectives: 23.6 us -> none  [local(): summed = lax.psum(partial_value, 'expert').astype(jnp.bfloat16)]
    reshape x2 -> x1, local copies, waits for them, and re-layouts: 6.91 us -> 2.73 us  [local(): gathered.reshape(dp_count, ctx_count, seq_count, ctx_count, group_count,...]
    transpose x0 -> x1, local copies, waits for them, and re-layouts: none -> 4.17 us  [local(): jnp.transpose(gathered, (0, 3, 4, 2, 5, 1, 6))]
    convert_element_type x0 -> x1, local copies, waits for them, and re-layouts: none -> 2.82 us  [local(): normed = (flat * scale * moe_gain[None, :]).astype(jnp.bfloat16)]
    reduce_sum x0 -> x1, other arithmetic: none -> 2.52 us  [local(): jnp.sum(lax.all_gather(partial_value, axis_name='expert'), axis=0)]
    all_gather x1, waiting for transfers between devices: 26.2 us -> 28.7 us  [local(): gathered = lax.all_gather(summed[None], ('dp', 'ctx'), axis=0, tiled=True)]
  transfers between devices with their start and end apart: 2 -> 3, of which waited for: 1 -> 2; matrix products, arithmetic and copies ran while one was open for 1% -> 1% of each run, Pallas kernels for 0% -> 0%
where the time goes in v1:
time: 213 us; the launch traced here: 212 us
  blocking collectives  85 us (40%)
  waiting for transfers between devices  60.2 us (28%)
  local copies, waits for them, and re-layouts  21.4 us (10%)
  matrix products  19.9 us (9%)
  between operations  13.9 us (7%)
  other arithmetic  11.3 us (5%)
    all_gather x1, blocking collectives, local(): routes = lax.all_gather(route[None], ALL_AXES, axis=0, tiled=True)  71.7 us
    all_gather x1, waiting for transfers between devices, local(): lax.all_gather(partial_value, axis_name='expert')  31.4 us
    all_gather x1, waiting for transfers between devices, local(): gathered = lax.all_gather(summed[None], ('dp', 'ctx'), axis=0, tiled=True)  28.7 us
    all_gather x1, blocking collectives, local(): decay_all = lax.all_gather(decay_log, 'ctx', axis=1, tiled=True)  13.3 us
    dot_general x1, matrix products, expert_ffn(): jnp.einsum('gfd,qd->gfq', gate_up[0], slot_rows, preferred_element_type=j...  10.5 us
    dot_general x1, matrix products, mixer(): ssd = jnp.einsum('sktuh,skuhp->skthp', kernel, x_float, precision=highest)  4.78 us
  transfers between devices with their start and end apart: 3, of which 2 were waited for; matrix products, arithmetic and copies ran while one was open for 1% of the time, Pallas kernels for 0%

profile of v1, /device:TPU:0, one launch (start us, length us, event | category | flops | bytes accessed | tf_op | source)
XLA Modules:
  0.0 212.2 jit_solution(2830134750785641175)
XLA Ops:
  7.2 0.0 all-gather.7.cloned.1.call-start
  7.2 1.7 pad_maximum_fusion
  8.9 0.0 all-gather.7.cloned.1.call-update
  9.0 0.0 all-gather.9.cloned.1.call-start
  9.0 0.7 pad_add_fusion
  9.7 71.7 %all-gather = s32[64,4,2,2]{1,2,0,3:T(2,128)S(1)} all-gather(s32[2,4,2,2]{1,2,0,3:T(2,128)S(1)} %pad_add_fusion), channel_id=2, replica_groups=mesh['dp'=2,'ctx'=4,'expert'=4] {'dp','ctx','expert'}, dimensions={0}, use_global_device_ids=true | all-gather | bytes 4224 | tf_op jit(solution)/shard_map/all_gather | solution.py:105
  81.4 13.3 %all_gather.19 = f32[2,64,32]{2,1,0:T(8,128)S(1)} all-gather(f32[2,16,32]{2,1,0:T(8,128)} %param.15), channel_id=1, replica_groups=mesh['dp'=2,'ctx'=4,'expert'=4] {'ctx'}, dimensions={1}, use_global_device_ids=true | all-gather | bytes 20480 | tf_op jit(solution)/shard_map/all_gather | solution.py:103
  94.8 0.0 all-gather.7.cloned.1.call-done
  94.8 0.9 fusion.37
  95.7 1.2 fusion.42
  96.9 0.1 reduce_window_sum.11
  97.0 0.1 copy.53
  97.1 0.0 copy-start.2
  97.1 1.3 copy.65
  98.4 0.6 copy.66
  99.0 0.0 copy-done.2
  99.0 4.8 %bitcast_add_fusion = f32[2,1,64,32,64]{2,4,3,0,1:T(8,128)} fusion(f32[2,1,64,32,64]{2,4,3,0,1:T(8,128)S(1)} %bitcast.44, bf16[2,64,32,64]{1,3,2,0:T(8,128)(2,1)} %bitcast.47, f32[32]{0:T(128)S(1)} %copy-done.2, f32[2,64,64]{2,1,0:T(8,128)S(1)} %fusion.37, f32[2,64,32]{1,2,0:T(8,128)S(1)} %copy.53, pred[64,64]{1,0:T(8,128)(4,1)S(1)} %iota_compare_fusion.1), kind=kOutput, calls=%fused_computation.11 | convolution fusion | flops 202899456 | bytes 2674816 | tf_op jit(solution)/shard_map/sktuh,skuhp->skthp/dot_general | solution.py:25
  103.8 0.0 copy-start
  103.8 2.3 %copy.67 = f32[2,64,2048]{2,1,0:T(8,128)S(1)} copy(f32[2,64,2048]{1,2,0:T(8,128)} %bitcast.45) | data formatting | bytes 2097152 | tf_op jit(solution)/shard_map/reshape | solution.py:45
  106.1 0.0 copy-done
  106.1 3.8 %fusion.6 = f32[2,64,1024]{2,1,0:T(8,128)} fusion(bf16[2048,1024]{1,0:T(8,128)(2,1)} %param.17, f32[2,64,2048]{2,1,0:T(8,128)S(1)} %copy.67, bf16[2,64,4352]{2,1,0:T(8,128)(2,1)S(1)} %copy-done), kind=kOutput, calls=%fused_computation.9 | convolution fusion | flops 538705920 | bytes 6291456 | tf_op jit(solution)/shard_map/stk,kd->std/dot_general | solution.py:113
  109.9 0.0 copy-start.1
  109.9 0.0 all-gather.9.cloned.1.call-update
  109.9 0.2 all-gather.11.cloned.1.call-start
  110.1 31.4 %all-gather.9.cloned.1.call-done = f32[8,64,1024]{2,1,0:T(8,128)} async-done(((f32[2,64,1024]{2,1,0:T(8,128)}), f32[8,64,1024]{2,1,0:T(8,128)}) %all-gather.9.cloned.1.call-update) | async-done | bytes 2097168 | tf_op jit(solution)/shard_map/all_gather | solution.py:116
  141.6 2.5 %reduce_sum.18 = bf16[2,64,1024]{2,1,0:T(8,128)(2,1)} reduce(f32[4,2,64,1024]{3,2,1,0:T(8,128)} %bitcast.43, f32[]{:T(128)} %constant.14.clone.1), dimensions={0}, to_apply=%region_1.2 | reduce | flops 393216 | bytes 2359300 | tf_op jit(solution)/shard_map/reduce_sum | solution.py:116
  144.1 0.0 all-gather.11.cloned.1.call-update
  144.1 0.0 copy-done.1
  144.2 0.1 copy.59
  144.3 0.1 copy.60
  144.4 0.1 copy.62
  144.5 0.2 fusion.34
  144.8 28.7 %all-gather.11.cloned.1.call-done = bf16[16,64,1024]{2,1,0:T(8,128)(2,1)} async-done(((bf16[2,64,1024]{2,1,0:T(8,128)(2,1)}), bf16[16,64,1024]{2,1,0:T(8,128)(2,1)}) %all-gather.11.cloned.1.call-update) | async-done | bytes 2097168 | tf_op jit(solution)/shard_map/all_gather | solution.py:117
  173.4 2.7 %reshape.139 = bf16[2,4,2,4,4,4,1024]{6,5,4,3,2,1,0:T(4,128)(2,1)S(1)} reshape(bf16[16,64,1024]{2,1,0:T(8,128)(2,1)} %all-gather.11.cloned.1.call-done) | data formatting | bytes 4194304 | tf_op jit(solution)/shard_map/reshape | solution.py:118
  176.2 1.2 fusion.3
  177.4 1.9 fusion.5
  179.3 2.8 %copy.63 = bf16[2,4,4,2,4,4,1024]{6,5,4,3,2,1,0:T(4,128)(2,1)S(1)} copy(bf16[2,4,4,2,4,4,1024]{6,4,2,1,3,5,0:T(4,128)(2,1)S(1)} %fusion.5) | data formatting | bytes 4194304 | tf_op jit(solution)/shard_map/convert_element_type | solution.py:132
  182.1 2.2 %copy.68 = bf16[32,8,4,1024]{3,1,2,0:T(8,128)(2,1)} copy(bf16[32,8,4,1024]{3,2,1,0:T(4,128)(2,1)S(1)} %bitcast.42) | data formatting | bytes 4194304
  184.3 10.5 %fusion.16 = f32[2,896,256]{1,2,0:T(8,128)} fusion(bf16[1,2,896,4096]{3,2,1,0:T(8,128)(2,1)} %param.19, bf16[256,4096]{1,0:T(8,128)(2,1)} %bitcast.46, pred[32,8,256]{2,1,0:T(8,128)(4,1)S(1)} %fusion.34), kind=kOutput, calls=%fused_computation.18 | convolution fusion | flops 4296015872 | bytes 18677760 | tf_op jit(solution)/shard_map/gfd,qd->gfq/dot_general | solution.py:49
  194.8 1.7 fusion.29
  196.5 1.0 copy.64
  197.5 4.2 %copy.58 = bf16[2,4,4,2,4,4,1024]{6,5,4,3,2,1,0:T(4,128)(2,1)} copy(bf16[2,4,4,2,4,4,1024]{6,4,2,1,3,5,0:T(4,128)(2,1)S(1)} %bitcast.41) | data formatting | bytes 4194304 | tf_op jit(solution)/shard_map/transpose | solution.py:121
  201.7 3.3 %reshape.140 = bf16[32,8,4096]{2,1,0:T(8,128)(2,1)S(1)} reshape(bf16[2,4,4,2,4,4,1024]{6,5,4,3,2,1,0:T(4,128)(2,1)} %copy.58) | data formatting | bytes 4194304 | tf_op jit(solution)/shard_map/reshape | solution.py:121
  205.0 0.7 reshape.141
  (8 shorter events, 0.1 us)
Async XLA Ops:
  7.2 87.6 %all-gather.7.cloned.1.call-start = ((), (), s32[]{:S(2)}) async-start(), calls=%async_computation | async-start | bytes 1392640 | tf_op jit(solution)/shard_map/all_gather | solution.py:102
  9.0 132.6 %all-gather.9.cloned.1.call-start = ((), (), s32[]{:S(2)}) async-start(), calls=%async_computation.1 | async-start | bytes 2621440 | tf_op jit(solution)/shard_map/all_gather | solution.py:116
  97.1 1.9 copy-start.2
  103.8 2.3 %copy-start = (bf16[2,64,4352]{2,1,0:T(8,128)(2,1)S(1)}, bf16[2,64,4352]{2,1,0:T(8,128)(2,1)}, u32[]{:S(2)}) copy-start(bf16[2,64,4352]{2,1,0:T(8,128)(2,1)} %all-gather.7.cloned.1.call-done) | copy-start | bytes 3342340
  109.9 34.3 %copy-start.1 = (f32[4096]{0:T(1024)S(1)}, f32[4096]{0:T(1024)}, u32[]{:S(2)}) copy-start(f32[4096]{0:T(1024)} %param.18) | copy-start | bytes 49156
  109.9 63.5 %all-gather.11.cloned.1.call-start = ((), (), s32[]{:S(2)}) async-start(), calls=%async_computation.2 | async-start | bytes 2359296 | tf_op jit(solution)/shard_map/all_gather | solution.py:117
Sparse Core Ops, SparseCore 0:
  10.1 32.3 all-gather.6
  110.0 31.5 all-gather.8
  144.2 29.1 all-gather.10
